TPU v7x, 512 devices: a whole 4x8x8 slice. The times are simulated.
512 devices in a mesh: req: 128 (over z, y, core), grp: 4 (over x).
Axes of the slice: x: 4, y: 8, z: 8, core: 2. Of those that a mesh axis runs over, the one named last changes fastest.
Arguments:
- owner_slab: bfloat16 [65536, 1024], P('req'), may hold values from -6 to 6
- segment_ids: int32 [128, 512], P('req'), may hold values from 0 to 511, as said below
- head_weights: bfloat16 [1024, 16, 192], P(None, 'grp')
- merge_weights: bfloat16 [16, 64, 1024], P('grp'), may hold values from -0.1875 to 0.1875
- first_gain: float32 [1024], replicated, may hold values from 0.25 to 1.75
- first_bias: float32 [1024], replicated, may hold values from -3 to 3
- up_weights: bfloat16 [1024, 4096], P('req', 'grp'), may hold values from -0.1875 to 0.1875
- down_weights: bfloat16 [4096, 1024], P('grp', 'req'), may hold values from -0.09375 to 0.09375
- second_gain: float32 [1024], replicated, may hold values from 0.25 to 1.75
- second_bias: float32 [1024], replicated, may hold values from -3 to 3
- page_table: int32 [128, 4], P('req'), may hold values from 0 to 3, each once within a row
- row_map: int32 [128, 4, 128], P('req', 'grp'), may hold values from 0 to 127, each once within a row
Outputs:
- layer_out: bfloat16 [65536, 1024], P(('req', 'grp'))
- cache_pages: bfloat16 [512, 128, 16, 128], P('req', None, 'grp')
Inputs may be any that keep to these rules, and one draw needn't show every extreme that they name: `segment_ids`: within each slab the ids start at 0, never fall and rise by at most one from row to row; in one slab all 512 rows form a single request, and in one other slab every row is a request of its own.
All inputs are finite; a program needn't handle non-finite values.
Results may differ from a plain program's by a relative error of at most 0.0075.
Values may be sent and summed in bfloat16 or wider, within the bound.
No kernel may reach another device: no remote copies, remote signals or barrier semaphores. Data moves between devices by JAX's collectives and lax.ppermute only.
A program may use at most 64 MiB of HBM per device.

v0:
```python
import math
import jax
import jax.numpy as jnp
from jax import lax
from jax.sharding import PartitionSpec as P

EPSILON = 1e-05


def layer_norm(values, gain, bias):
    center = values - jnp.mean(values, axis=-1, keepdims=True)
    spread = jnp.mean(center * center, axis=-1, keepdims=True)
    return center * lax.rsqrt(spread + EPSILON) * gain + bias


def local(
    owner_slab,
    segment_ids,
    head_weights,
    merge_weights,
    first_gain,
    first_bias,
    up_weights,
    down_weights,
    second_gain,
    second_bias,
    page_table,
    row_map,
):
    group = lax.axis_size("grp")
    owners = lax.axis_size("req")
    rows_all = owner_slab.shape[0]
    width = owner_slab.shape[1]
    quarter = rows_all // group
    local_heads = head_weights.shape[1]
    head_dim = head_weights.shape[2] // 3
    projected = jnp.einsum(
        "nd,dhc->nhc", owner_slab, head_weights, preferred_element_type=jnp.float32
    ).astype(jnp.bfloat16)
    queries = jnp.moveaxis(projected[:, :, :head_dim], 1, 0)
    key_rows = jnp.moveaxis(projected[:, :, head_dim : 2 * head_dim], 1, 0)
    value_rows = jnp.moveaxis(projected[:, :, 2 * head_dim :], 1, 0)
    segment = segment_ids[0]
    position = jnp.arange(rows_all, dtype=jnp.int32)
    allowed = (position[:, None] >= position[None, :]) & (segment[:, None] == segment[None, :])
    scale = 1.0 / math.sqrt(head_dim)

    def one_head(operands):
        query_head, key_head, value_head = operands
        scores = (
            lax.dot_general(
                query_head, key_head, (((1,), (1,)), ((), ())), preferred_element_type=jnp.float32
            )
            * scale
        )
        scores = jnp.where(allowed, scores, -1e30)
        probs = jax.nn.softmax(scores, axis=-1).astype(jnp.bfloat16)
        return jnp.dot(probs, value_head, preferred_element_type=jnp.float32).astype(jnp.bfloat16)

    attended = jnp.moveaxis(lax.map(one_head, (queries, key_rows, value_rows)), 0, 1)
    own = lax.axis_index("grp")
    own_rows = lax.dynamic_slice_in_dim(owner_slab, own * quarter, quarter, 0).astype(jnp.float32)
    partial_rows = jnp.einsum(
        "nhd,hde->ne", attended, merge_weights, preferred_element_type=jnp.float32
    )
    mixed = lax.psum_scatter(partial_rows, "grp", scatter_dimension=0, tiled=True)
    hidden = layer_norm(own_rows + mixed, first_gain, first_bias).astype(jnp.bfloat16)
    slots = quarter // owners
    placed = jnp.zeros_like(hidden).at[row_map[0, 0]].set(hidden)
    arrived = lax.all_to_all(
        placed.reshape(owners, slots, width), "req", split_axis=0, concat_axis=0, tiled=True
    )
    even_rows = arrived.reshape(quarter, width)
    group_rows = lax.all_gather(even_rows, "grp", axis=0, tiled=True)
    raised = jnp.dot(
        group_rows,
        lax.all_gather(up_weights, "req", axis=0, tiled=True),
        preferred_element_type=jnp.float32,
    )
    activated = jax.nn.gelu(raised, approximate=False).astype(jnp.bfloat16)
    lowered_all = jnp.dot(
        activated,
        lax.all_gather(down_weights, "req", axis=1, tiled=True),
        preferred_element_type=jnp.float32,
    )
    lowered = lax.psum_scatter(lowered_all, "grp", scatter_dimension=0, tiled=True)
    layer_out = layer_norm(
        even_rows.astype(jnp.float32) + lowered, second_gain, second_bias
    ).astype(jnp.bfloat16)
    page_count = page_table.shape[1]
    page_rows = rows_all // page_count
    stacked = projected[:, :, head_dim:].reshape(page_count, page_rows, local_heads, 2 * head_dim)
    cache_pages = jnp.zeros_like(stacked).at[page_table[0]].set(stacked)
    return (layer_out, cache_pages)


def solution(mesh):
    in_specs = (
        P("req", None),
        P("req", None),
        P(None, "grp", None),
        P("grp", None, None),
        P(),
        P(),
        P("req", "grp"),
        P("grp", "req"),
        P(),
        P(),
        P("req", None),
        P("req", "grp", None),
    )
    out_specs = (P(("req", "grp"), None), P("req", None, "grp", None))
    return jax.shard_map(local, mesh=mesh, in_specs=in_specs, out_specs=out_specs, check_vma=False)
```

profile of v0, /device:TPU:1, one launch (start us, length us, event | category | flops | bytes accessed | tf_op | source)
XLA Modules:
  0.0 281.3 jit_solution(15280526608803334837)
XLA Ops:
  8.1 1.3 copy-done
  9.4 2.2 fusion.105
  11.9 0.5 copy-done.7
  12.3 3.7 %while.11 = (s32[]{:T(128)}, bf16[4,512,64]{1,2,0:T(8,128)(2,1)S(1)}, bf16[4,512,64]{1,2,0:T(8,128)(2,1)S(1)}, bf16[4,512,64]{1,2,0:T(8,128)(2,1)S(1)}, bf16[4,5...) while((s32[]{:T(128)}, bf16[4,512,64]{1,2,0:T(8,128)(2,1)S(1)}, ...), condition=%wide.region_3.4_spmd.clone, body=%wide.region_0.3_spmd.clone.sunk | while | flops 70024192 | bytes 3424341 | solution.py:60
  12.3 0.4 fusion.116
  12.9 0.3 fusion.118
  13.3 0.4 fusion.116
  14.2 0.4 fusion.116
  15.1 0.4 fusion.116
  16.1 0.7 copy-done.10
  16.8 3.0 %convolution_bitcast_fusion = f32[512,1024]{1,0:T(8,128)} fusion(bf16[4,64,1024]{2,1,0:T(8,128)(2,1)} %param.17, bf16[4,512,64]{1,2,0:T(8,128)(2,1)} %copy-done.10), kind=kOutput, calls=%fused_computation.40 | convolution fusion | flops 268435456 | bytes 2883584 | tf_op jit(solution)/shard_map/nhd,hde->ne/dot_general | solution.py:63
  19.9 0.5 all-gather.5.cloned.1.call-update
  20.4 0.5 all-gather.7.cloned.1.call-update
  21.1 39.4 %reduce-scatter.3.cloned.1.call-done = f32[128,1024]{1,0:T(8,128)} async-done(((f32[512,1024]{1,0:T(8,128)}), f32[128,1024]{1,0:T(8,128)}) %reduce-scatter.3.cloned.1.call-update) | async-done | bytes 524304 | tf_op jit(solution)/shard_map/reduce_scatter | solution.py:66
  60.4 1.2 fusion.70
  61.6 1.2 multiply_reduce_fusion.1
  62.9 1.9 scatter_custom_fusion
  64.8 0.5 broadcast.106
  65.3 0.8 reduce
  66.3 30.1 %all_to_all.5 = bf16[128,2,512]{2,1,0:T(2,128)(2,1)S(1)} all-to-all(bf16[128,2,512]{2,1,0:T(2,128)(2,1)S(1)} %reshape.126), channel_id=1, replica_groups=mesh['req'=128,'grp'=4] {'req'}, dimensions={0} | all-to-all | bytes 524288 | tf_op jit(solution)/shard_map/all_to_all | solution.py:70
  96.6 0.8 copy.29
  97.7 16.5 %all-gather.5.cloned.1.call-done = bf16[1024,1024]{1,0:T(8,128)(2,1)} async-done(((bf16[8,1024]{1,0:T(8,128)(2,1)}), bf16[1024,1024]{1,0:T(8,128)(2,1)}) %all-gather.5.cloned.1.call-update) | async-done | bytes 2097168 | tf_op jit(solution)/shard_map/all_gather | solution.py:77
  114.2 82.0 %all-gather.7.cloned.1.call-done = bf16[1024,1024]{0,1:T(8,128)(2,1)} async-done(((bf16[1024,8]{0,1:T(8,128)(2,1)}), bf16[1024,1024]{0,1:T(8,128)(2,1)}) %all-gather.7.cloned.1.call-update) | async-done | bytes 2097168 | tf_op jit(solution)/shard_map/all_gather | solution.py:83
  196.1 26.4 %all-gather.9.cloned.1.call-done = bf16[512,1,1024]{2,0,1:T(8,128)(2,1)} async-done(((bf16[128,1,1024]{2,0,1:T(8,128)(2,1)}), bf16[512,1,1024]{2,0,1:T(8,128)(2,1)}) %all-gather.9.cloned.1.call-update) | async-done | bytes 1048592 | tf_op jit(solution)/shard_map/all_gather | solution.py:74
  222.5 10.1 %fusion.25 = f32[512,1024]{1,0:T(8,128)} fusion(bf16[1024,1024]{0,1:T(8,128)(2,1)} %all-gather.7.cloned.1.call-done, bf16[1024,1024]{1,0:T(8,128)(2,1)} %all-gather.5.cloned.1.call-done, bf16[512,1,1024]{2,0,1:T(8,128)(2,1)} %all-gather.9.cloned.1.call-done), kind=kOutput, calls=%fused_computation.41 | convolution fusion | flops 2181562368 | bytes 7340032 | tf_op jit(solution)/shard_map/dot_general | solution.py:81
  232.8 0.4 copy.31
  233.4 0.8 scatter_fusion
  234.2 1.2 copy.32
  235.4 34.8 %reduce-scatter.5.cloned.1.call-done = f32[128,1024]{1,0:T(8,128)} async-done(((f32[512,1024]{1,0:T(8,128)}), f32[128,1024]{1,0:T(8,128)}) %reduce-scatter.5.cloned.1.call-update) | async-done | bytes 524304 | tf_op jit(solution)/shard_map/reduce_scatter | solution.py:86
  270.2 1.3 fusion.69
  271.5 1.3 multiply_reduce_fusion
  272.8 0.9 add_convert_fusion
  (48 shorter events, 3.2 us)
Async XLA Ops:
  8.0 1.4 copy-start
  8.0 52.4 %reduce-scatter.3.cloned.1.call-start = ((), (), s32[]{:S(2)}) async-start(), calls=%async_computation.3 | async-start | bytes 2621440 | tf_op jit(solution)/shard_map/reduce_scatter | solution.py:66
  11.6 0.7 copy-start.7
  16.1 0.7 copy-start.10
  16.8 4.3 %copy-start.8 = (s32[1,1,128]{2,1,0:T(1,128)S(1)}, s32[1,1,128]{2,1,0:T(1,128)}, u32[]{:S(2)}) copy-start(s32[1,1,128]{2,1,0:T(1,128)} %param.25) | copy-start | bytes 1540
  16.8 43.6 %copy-start.2 = (bf16[512,1024]{1,0:T(8,128)(2,1)S(1)}, bf16[512,1024]{1,0:T(8,128)(2,1)}, u32[]{:S(2)}) copy-start(bf16[512,1024]{1,0:T(8,128)(2,1)} %param.14) | copy-start | bytes 3145732
  19.8 43.1 %copy-start.3 = (f32[1024]{0:T(1024)S(1)}, f32[1024]{0:T(1024)}, u32[]{:S(2)}) copy-start(f32[1024]{0:T(1024)} %param.19) | copy-start | bytes 12292
  19.8 43.1 %copy-start.4 = (f32[1024]{0:T(1024)S(1)}, f32[1024]{0:T(1024)}, u32[]{:S(2)}) copy-start(f32[1024]{0:T(1024)} %param.18) | copy-start | bytes 12292
  19.8 94.3 %all-gather.5.cloned.1.call-start = ((), (), s32[]{:S(2)}) async-start(), calls=%async_computation.4 | async-start | bytes 2113536 | tf_op jit(solution)/shard_map/all_gather | solution.py:77
  20.4 175.7 %all-gather.7.cloned.1.call-start = ((), (), s32[]{:S(2)}) async-start(), calls=%async_computation.5 | async-start | bytes 2113536 | tf_op jit(solution)/shard_map/all_gather | solution.py:83
  21.0 201.5 %all-gather.9.cloned.1.call-start = ((), (), s32[]{:S(2)}) async-start(), calls=%async_computation.7 | async-start | bytes 1310720 | tf_op jit(solution)/shard_map/all_gather | solution.py:74
  97.4 172.8 %reduce-scatter.5.cloned.1.call-start = ((), (), s32[]{:S(2)}) async-start(), calls=%async_computation.6 | async-start | bytes 2621440 | tf_op jit(solution)/shard_map/reduce_scatter | solution.py:86
  232.6 0.7 copy-start.9
  233.4 39.4 %copy-start.5 = (f32[1024]{0:T(1024)S(1)}, f32[1024]{0:T(1024)}, u32[]{:S(2)}) copy-start(f32[1024]{0:T(1024)} %param.23) | copy-start | bytes 12292
  233.4 39.4 %copy-start.6 = (f32[1024]{0:T(1024)S(1)}, f32[1024]{0:T(1024)}, u32[]{:S(2)}) copy-start(f32[1024]{0:T(1024)} %param.22) | copy-start | bytes 12292
  270.2 2.6 copy-start.1
Sparse Core Ops, SparseCore 0:
  19.9 40.4 reduce-scatter.2
  232.8 37.4 reduce-scatter.4
Sparse Core Ops, SparseCore 1:
  23.4 90.7 all-gather.4
  117.2 78.9 all-gather.6
  198.7 23.8 all-gather.8
where the time goes:
time: 282 us; the launch traced here: 281 us
  waiting for transfers between devices  200 us (71%)
  blocking collectives  30.1 us (11%)
  matrix products  18.2 us (6%)
  between operations  15.9 us (6%)
  other arithmetic  9.46 us (3%)
  local copies, waits for them, and re-layouts  7.03 us (2%)
    all_gather x1, waiting for transfers between devices, local(): lax.all_gather(down_weights, 'req', axis=1, tiled=True)  82 us
    reduce_scatter x1, waiting for transfers between devices, local(): lax.psum_scatter(partial_rows, 'grp', scatter_dimension=0, tiled=True)  39.4 us
    reduce_scatter x1, waiting for transfers between devices, local(): lax.psum_scatter(lowered_all, 'grp', scatter_dimension=0, tiled=True)  34.8 us
    all_to_all x1, blocking collectives, local(): lax.all_to_all(placed.reshape(owners, slots, width), 'req', split_axis=0,...  30.1 us
    all_gather x1, waiting for transfers between devices, local(): group_rows = lax.all_gather(even_rows, 'grp', axis=0, tiled=True)  26.4 us
    all_gather x1, waiting for transfers between devices, local(): lax.all_gather(up_weights, 'req', axis=0, tiled=True)  16.5 us
    dot_general x1, matrix products, local(): jnp.dot(activated, lax.all_gather(down_weights, 'req', axis=1, tiled=True...  10.1 us
  transfers between devices with their start and end apart: 5, of which 5 were waited for; matrix products, arithmetic and copies ran while one was open for 3% of the time, Pallas kernels for 0%

commit v1 on v0

--- a/solution.py
+++ b/solution.py
@@ -3,6 +3,7 @@
 import jax.numpy as jnp
 from jax import lax
 from jax.sharding import PartitionSpec as P
+from jax.lax import all_to_all, psum
 
 EPSILON = 1e-05
 
@@ -71,7 +72,9 @@
         placed.reshape(owners, slots, width), "req", split_axis=0, concat_axis=0, tiled=True
     )
     even_rows = arrived.reshape(quarter, width)
-    group_rows = lax.all_gather(even_rows, "grp", axis=0, tiled=True)
+    group_rows = jnp.concatenate(
+        all_to_all(jnp.stack([even_rows] * psum(1, "grp")), "grp", 0, 0), axis=0
+    )
     raised = jnp.dot(
         group_rows,
         lax.all_gather(up_weights, "req", axis=0, tiled=True),

time: 282 us -> 249 us (0.88)
  waiting for transfers between devices: 200 us -> 163 us
  starting transfers between devices: 0.38 us -> 4.6 us
    all_gather x1 -> x0, waiting for transfers between devices: 26.4 us -> none  [local(): group_rows = lax.all_gather(even_rows, 'grp', axis=0, tiled=True)]
    reduce_scatter x1, waiting for transfers between devices: 34.8 us -> 28.9 us  [local(): lax.psum_scatter(lowered_all, 'grp', scatter_dimension=0, tiled=True)]
    all_gather x1, waiting for transfers between devices: 16.5 us -> 11.8 us  [local(): lax.all_gather(up_weights, 'req', axis=0, tiled=True)]
    all_to_all x0 -> x1, starting transfers between devices: none -> 4.25 us  [local(): all_to_all(jnp.stack([even_rows] * psum(1, 'grp')), 'grp', 0, 0)]
  transfers between devices with their start and end apart: 5 -> 5, of which waited for: 5 -> 4; matrix products, arithmetic and copies ran while one was open for 3% -> 4% of each run, Pallas kernels for 0% -> 0%
where the time goes in v1:
time: 249 us
  waiting for transfers between devices  163 us (65%)
  blocking collectives  30.1 us (12%)
  matrix products  18.2 us (7%)
  between operations  15.7 us (6%)
  other arithmetic  9.46 us (4%)
  local copies, waits for them, and re-layouts  7.44 us (3%)
  starting transfers between devices  4.6 us (2%)
    all_gather x1, waiting for transfers between devices, local(): lax.all_gather(down_weights, 'req', axis=1, tiled=True)  82 us
    reduce_scatter x1, waiting for transfers between devices, local(): lax.psum_scatter(partial_rows, 'grp', scatter_dimension=0, tiled=True)  39.4 us
    all_to_all x1, blocking collectives, local(): lax.all_to_all(placed.reshape(owners, slots, width), 'req', split_axis=0,...  30.1 us
    reduce_scatter x1, waiting for transfers between devices, local(): lax.psum_scatter(lowered_all, 'grp', scatter_dimension=0, tiled=True)  28.9 us
    all_gather x1, waiting for transfers between devices, local(): lax.all_gather(up_weights, 'req', axis=0, tiled=True)  11.8 us
    dot_general x1, matrix products, local(): jnp.dot(activated, lax.all_gather(down_weights, 'req', axis=1, tiled=True...  10.1 us
  transfers between devices with their start and end apart: 5, of which 4 were waited for; matrix products, arithmetic and copies ran while one was open for 4% of the time, Pallas kernels for 0%

profile of v1, /device:TPU:1, one launch (start us, length us, event | category | flops | bytes accessed | tf_op | source)
XLA Modules:
  0.0 248.8 jit_solution(9820498936093790334)
XLA Ops:
  8.1 1.3 copy-done
  9.4 2.2 fusion.101
  11.9 0.5 copy-done.7
  12.3 3.7 %while.11 = (s32[]{:T(128)}, bf16[4,512,64]{1,2,0:T(8,128)(2,1)S(1)}, bf16[4,512,64]{1,2,0:T(8,128)(2,1)S(1)}, bf16[4,512,64]{1,2,0:T(8,128)(2,1)S(1)}, bf16[4,5...) while((s32[]{:T(128)}, bf16[4,512,64]{1,2,0:T(8,128)(2,1)S(1)}, ...), condition=%wide.region_3.4_spmd.clone, body=%wide.region_0.3_spmd.clone.sunk | while | flops 70024192 | bytes 3424341 | solution.py:61
  12.3 0.4 fusion.113
  12.9 0.3 fusion.115
  13.3 0.4 fusion.113
  14.2 0.4 fusion.113
  15.1 0.4 fusion.113
  16.1 0.7 copy-done.10
  16.8 3.0 %convolution_bitcast_fusion = f32[512,1024]{1,0:T(8,128)} fusion(bf16[4,64,1024]{2,1,0:T(8,128)(2,1)} %param.17, bf16[4,512,64]{1,2,0:T(8,128)(2,1)} %copy-done.10), kind=kOutput, calls=%fused_computation.40 | convolution fusion | flops 268435456 | bytes 2883584 | tf_op jit(solution)/shard_map/nhd,hde->ne/dot_general | solution.py:64
  19.9 0.5 all-gather.3.cloned.1.call-update
  20.4 0.5 all-gather.5.cloned.1.call-update
  21.0 39.4 %reduce-scatter.3.cloned.1.call-done = f32[128,1024]{1,0:T(8,128)} async-done(((f32[512,1024]{1,0:T(8,128)}), f32[128,1024]{1,0:T(8,128)}) %reduce-scatter.3.cloned.1.call-update) | async-done | bytes 524304 | tf_op jit(solution)/shard_map/reduce_scatter | solution.py:67
  60.4 1.2 fusion.64
  61.6 1.2 multiply_reduce_fusion.1
  62.9 1.9 scatter_custom_fusion
  64.8 0.5 broadcast.107
  65.3 0.8 reduce
  66.3 30.1 %all_to_all.10 = bf16[128,2,512]{2,1,0:T(2,128)(2,1)S(1)} all-to-all(bf16[128,2,512]{2,1,0:T(2,128)(2,1)S(1)} %reshape.130), channel_id=1, replica_groups=mesh['req'=128,'grp'=4] {'req'}, dimensions={0} | all-to-all | bytes 524288 | tf_op jit(solution)/shard_map/all_to_all | solution.py:71
  96.7 1.1 stack.3
  97.8 4.3 %all-to-all-start.1 = ((bf16[4,128,1024]{2,1,0:T(8,128)(2,1)}), bf16[4,128,1024]{2,1,0:T(8,128)(2,1)}, u32[]{:S(2)}, u32[]{:S(2)}) async-start(bf16[4,128,1024]{2,1,0:T(8,128)(2,1)} %stack.3), calls=%async_computation.2 | async-start | bytes 2097152 | tf_op jit(solution)/shard_map/all_to_all | solution.py:76
  102.3 11.8 %all-gather.3.cloned.1.call-done = bf16[1024,1024]{1,0:T(8,128)(2,1)} async-done(((bf16[8,1024]{1,0:T(8,128)(2,1)}), bf16[1024,1024]{1,0:T(8,128)(2,1)}) %all-gather.3.cloned.1.call-update) | async-done | bytes 2097168 | tf_op jit(solution)/shard_map/all_gather | solution.py:80
  114.2 82.0 %all-gather.5.cloned.1.call-done = bf16[1024,1024]{0,1:T(8,128)(2,1)} async-done(((bf16[1024,8]{0,1:T(8,128)(2,1)}), bf16[1024,1024]{0,1:T(8,128)(2,1)}) %all-gather.5.cloned.1.call-update) | async-done | bytes 2097168 | tf_op jit(solution)/shard_map/all_gather | solution.py:86
  196.1 10.1 %fusion.25 = f32[512,1024]{1,0:T(8,128)} fusion(bf16[1024,1024]{0,1:T(8,128)(2,1)} %all-gather.5.cloned.1.call-done, bf16[512,1024]{1,0:T(8,128)(2,1)} %bitcast.11, bf16[1024,1024]{1,0:T(8,128)(2,1)} %all-gather.3.cloned.1.call-done), kind=kOutput, calls=%fused_computation.41 | convolution fusion | flops 2181562368 | bytes 7340032 | tf_op jit(solution)/shard_map/dot_general | solution.py:84
  206.4 0.4 copy.28
  207.1 0.8 scatter_fusion
  207.8 1.2 copy.29
  209.0 28.9 %reduce-scatter.5.cloned.1.call-done = f32[128,1024]{1,0:T(8,128)} async-done(((f32[512,1024]{1,0:T(8,128)}), f32[128,1024]{1,0:T(8,128)}) %reduce-scatter.5.cloned.1.call-update) | async-done | bytes 524304 | tf_op jit(solution)/shard_map/reduce_scatter | solution.py:89
  237.9 1.3 fusion.63
  239.2 1.3 multiply_reduce_fusion
  240.5 0.9 add_convert_fusion
  (48 shorter events, 3.2 us)
Async XLA Ops:
  8.0 1.4 copy-start
  8.0 52.4 %reduce-scatter.3.cloned.1.call-start = ((), (), s32[]{:S(2)}) async-start(), calls=%async_computation.4 | async-start | bytes 2621440 | tf_op jit(solution)/shard_map/reduce_scatter | solution.py:67
  11.6 0.7 copy-start.7
  16.1 0.7 copy-start.10
  16.8 4.2 %copy-start.8 = (s32[1,1,128]{2,1,0:T(1,128)S(1)}, s32[1,1,128]{2,1,0:T(1,128)}, u32[]{:S(2)}) copy-start(s32[1,1,128]{2,1,0:T(1,128)} %param.25) | copy-start | bytes 1540
  16.8 43.6 %copy-start.2 = (bf16[512,1024]{1,0:T(8,128)(2,1)S(1)}, bf16[512,1024]{1,0:T(8,128)(2,1)}, u32[]{:S(2)}) copy-start(bf16[512,1024]{1,0:T(8,128)(2,1)} %param.14) | copy-start | bytes 3145732
  19.8 43.1 %copy-start.3 = (f32[1024]{0:T(1024)S(1)}, f32[1024]{0:T(1024)}, u32[]{:S(2)}) copy-start(f32[1024]{0:T(1024)} %param.19) | copy-start | bytes 12292
  19.8 43.1 %copy-start.4 = (f32[1024]{0:T(1024)S(1)}, f32[1024]{0:T(1024)}, u32[]{:S(2)}) copy-start(f32[1024]{0:T(1024)} %param.18) | copy-start | bytes 12292
  19.8 94.4 %all-gather.3.cloned.1.call-start = ((), (), s32[]{:S(2)}) async-start(), calls=%async_computation.5 | async-start | bytes 2113536 | tf_op jit(solution)/shard_map/all_gather | solution.py:80
  20.4 175.7 %all-gather.5.cloned.1.call-start = ((), (), s32[]{:S(2)}) async-start(), calls=%async_computation.6 | async-start | bytes 2113536 | tf_op jit(solution)/shard_map/all_gather | solution.py:86
  97.8 98.3 %all-to-all-start.1 = ((bf16[4,128,1024]{2,1,0:T(8,128)(2,1)}), bf16[4,128,1024]{2,1,0:T(8,128)(2,1)}, u32[]{:S(2)}, u32[]{:S(2)}) async-start(bf16[4,128,1024]{2,1,0:T(8,128)(2,1)} %stack.3), calls=%async_computation.2 | async-start | bytes 2097152 | tf_op jit(solution)/shard_map/all_to_all | solution.py:76
  102.1 135.8 %reduce-scatter.5.cloned.1.call-start = ((), (), s32[]{:S(2)}) async-start(), calls=%async_computation.7 | async-start | bytes 2621440 | tf_op jit(solution)/shard_map/reduce_scatter | solution.py:89
  206.3 0.7 copy-start.9
  207.0 33.5 %copy-start.5 = (f32[1024]{0:T(1024)S(1)}, f32[1024]{0:T(1024)}, u32[]{:S(2)}) copy-start(f32[1024]{0:T(1024)} %param.23) | copy-start | bytes 12292
  207.0 33.5 %copy-start.6 = (f32[1024]{0:T(1024)S(1)}, f32[1024]{0:T(1024)}, u32[]{:S(2)}) copy-start(f32[1024]{0:T(1024)} %param.22) | copy-start | bytes 12292
  237.9 2.6 %copy-start.1 = (f32[128,1024]{1,0:T(8,128)S(1)}, f32[128,1024]{1,0:T(8,128)}, u32[]{:S(2)}) copy-start(f32[128,1024]{1,0:T(8,128)} %reduce-scatter.5.cloned.1.call-done) | copy-start | bytes 1572868
Sparse Core Ops, SparseCore 0:
  19.9 40.4 reduce-scatter.2
  206.4 31.4 reduce-scatter.4
Sparse Core Ops, SparseCore 1:
  23.4 90.7 all-gather.2
  117.2 78.9 all-gather.4
